TPU v7x, 512 devices: a whole 4x8x8 slice. The times are simulated.
512 devices in a mesh: seq: 64 (over y, x, core), ch: 8 (over z).
Axes of the slice: x: 4, y: 8, z: 8, core: 2. Of those that a mesh axis runs over, the one named last changes fastest.
Arguments:
- signal: bfloat16 [1536, 32768], P('ch', 'seq'), may hold values from -16 to 16
- input_norm_gain: float32 [1536], P('ch'), may hold values from 0.25 to 1.75
- value_weight: bfloat16 [1536, 1536], P('seq', 'ch'), may hold values from -0.15625 to 0.15625
- gate_weight: bfloat16 [1536, 1536], P('seq', 'ch'), may hold values from -0.15625 to 0.15625
- depth_taps: float32 [31, 1536], P(None, 'ch'), may hold values from -1 to 1
- cotangent: bfloat16 [1536, 32768], P('ch', 'seq'), may hold values from -6 to 6
Outputs:
- output: bfloat16 [1536, 32768], P('ch', 'seq')
- signal_gradient: bfloat16 [1536, 32768], P('ch', 'seq')
- grad_value: float32 [1536, 1536], P('seq', 'ch')
- grad_gate: float32 [1536, 1536], P('seq', 'ch')
- grad_taps: float32 [31, 1536], P(None, 'ch')
- gain_gradient: float32 [1536], P('ch')
All inputs are finite; a program needn't handle non-finite values.
Results may differ from a plain program's by a relative error of at most 0.02.
Values may be sent and summed in bfloat16 or wider, within the bound.
No kernel may reach another device: no remote copies, remote signals or barrier semaphores. Data moves between devices by JAX's collectives and lax.ppermute only.
A program may use at most 64 MiB of HBM per device.

v0:
```python
import jax
import jax.numpy as jnp
from jax import lax
from jax.sharding import PartitionSpec as P


def extended(cells, sides, width):
    for axis, dim in sides:
        count = lax.axis_size(axis)
        ends = count - 1
        head = lax.slice_in_dim(cells, 0, width, axis=dim)
        tail = lax.slice_in_dim(cells, cells.shape[dim] - width, cells.shape[dim], axis=dim)
        cells = jnp.concatenate(
            [
                lax.ppermute(tail, axis, [(i, (i + 1) % count) for i in range(ends)]),
                cells,
                lax.ppermute(head, axis, [((i + 1) % count, i) for i in range(ends)]),
            ],
            axis=dim,
        )
    return cells


def standardize_rows(columns_in):
    values = columns_in.astype(jnp.float32)
    average = jnp.mean(values, 0, keepdims=True)
    centred = values - average
    spread = jnp.mean(centred * centred, 0, keepdims=True)
    inverse_deviation = lax.rsqrt(spread + 1e-05)
    return (centred * inverse_deviation, inverse_deviation)


def depthwise(padded, kernel):
    channels = padded.shape[0]
    result = lax.conv_general_dilated(
        padded[None],
        kernel,
        (1,),
        "VALID",
        dimension_numbers=("NCH", "OIH", "NCH"),
        feature_group_count=channels,
        precision=lax.Precision.HIGHEST,
    )
    return result[0]


def shards(signal, input_norm_gain, value_weight, gate_weight, depth_taps, cotangent):
    local_cols = signal.shape[0]
    seq_position = lax.axis_index("seq")
    channel_position = lax.axis_index("ch")
    reach = depth_taps.shape[0] // 2
    complete_signal = lax.all_gather(signal, "ch", axis=0, tiled=True)
    complete_gain = lax.all_gather(input_norm_gain, "ch", axis=0, tiled=True)
    centered_unit, inverse_deviation = standardize_rows(complete_signal)
    normalized_signal = (centered_unit * complete_gain[:, None]).astype(jnp.bfloat16)
    centered_unit_rows = lax.dynamic_slice_in_dim(
        centered_unit, channel_position * local_cols, local_cols, 0
    )
    stacked = jnp.concatenate([value_weight, gate_weight], 1)
    gathered = lax.all_gather(stacked, "seq", axis=0, tiled=True)
    mixed = lax.dot_general(
        gathered, normalized_signal, (((0,), (0,)), ((), ())), preferred_element_type=jnp.float32
    )
    value = mixed[:local_cols]
    gate = mixed[local_cols:]
    sig_gate = jax.nn.sigmoid(gate)
    glued = (value * sig_gate).astype(jnp.bfloat16)
    glued_pad = extended(glued, (("seq", 1),), reach).astype(jnp.float32)
    forward_kernel = depth_taps.T[:, None, :]
    pre = depthwise(glued_pad, forward_kernel)
    sig_pre = jax.nn.sigmoid(pre)
    output = (pre * sig_pre).astype(jnp.bfloat16)
    grad_pre = (cotangent.astype(jnp.float32) * sig_pre * (1.0 + pre * (1.0 - sig_pre))).astype(
        jnp.bfloat16
    )
    grad_pre_f = grad_pre.astype(jnp.float32)
    grad_pad = extended(grad_pre, (("seq", 1),), reach).astype(jnp.float32)
    grad_glued = depthwise(grad_pad, forward_kernel[:, :, ::-1])
    tap_partial = depthwise(glued_pad, grad_pre_f[:, None, :]).T
    grad_v = (grad_glued * sig_gate).astype(jnp.bfloat16)
    grad_g = (grad_glued * value * sig_gate * (1.0 - sig_gate)).astype(jnp.bfloat16)
    grad_both = jnp.concatenate([grad_v, grad_g], 0)
    weight_partial = lax.dot_general(
        normalized_signal, grad_both, (((1,), (1,)), ((), ())), preferred_element_type=jnp.float32
    )
    normed_term = jnp.dot(gathered, grad_both, preferred_element_type=jnp.float32)
    normalized_gradient = lax.psum_scatter(
        normed_term.astype(jnp.bfloat16), "ch", scatter_dimension=0, tiled=True
    ).astype(jnp.float32)
    scaled_signal = normalized_gradient * input_norm_gain[:, None]
    moments = jnp.concatenate(
        [
            jnp.sum(scaled_signal, 0, keepdims=True),
            jnp.sum(scaled_signal * centered_unit_rows, 0, keepdims=True),
        ],
        0,
    )
    moments = lax.psum(moments, "ch") * (1.0 / complete_signal.shape[0])
    inverse_rows = inverse_deviation
    signal_gradient = (
        inverse_rows * (scaled_signal - moments[0:1] - centered_unit_rows * moments[1:2])
    ).astype(jnp.bfloat16)
    gain_portion = jnp.sum(normalized_gradient * centered_unit_rows, 1)
    extra = jnp.concatenate([tap_partial, gain_portion[None]], 0)
    extra = jnp.pad(extra, ((0, 0), (0, weight_partial.shape[1] - extra.shape[1])))
    summed = lax.psum(jnp.concatenate([weight_partial, extra], 0), "seq")
    rows = value_weight.shape[0]
    weight_sums = lax.dynamic_slice_in_dim(summed, seq_position * rows, rows, 0)
    grad_value = weight_sums[:, :local_cols]
    grad_gate = weight_sums[:, local_cols:]
    taps_rows = depth_taps.shape[0]
    full_rows = weight_partial.shape[0]
    grad_taps = summed[full_rows : full_rows + taps_rows, :local_cols]
    gain_gradient = summed[full_rows + taps_rows, :local_cols]
    return (output, signal_gradient, grad_value, grad_gate, grad_taps, gain_gradient)


def solution(mesh):
    placed = (
        P("ch", "seq"),
        P("ch"),
        P("seq", "ch"),
        P("seq", "ch"),
        P(None, "ch"),
        P("ch", "seq"),
    )
    return jax.shard_map(
        shards,
        mesh=mesh,
        in_specs=placed,
        out_specs=(
            P("ch", "seq"),
            P("ch", "seq"),
            P("seq", "ch"),
            P("seq", "ch"),
            P(None, "ch"),
            P("ch"),
        ),
        check_vma=False,
    )
```

profile of v0, /device:TPU:25, one launch (start us, length us, event | category | flops | bytes accessed | tf_op | source)
XLA Modules:
  0.0 444.6 jit_solution(922992032706214905)
XLA Ops:
  7.2 0.7 all-gather.5.cloned.1.call-update
  8.0 1.4 pad_maximum_fusion.5
  9.5 1.3 dynamic-slice
  11.4 0.9 dynamic-update-slice
  12.3 19.7 %all-reduce.1 = f32[1536]{0:T(1024)S(1)} all-reduce(f32[1536]{0:T(1024)S(1)} %dynamic-update-slice), channel_id=1, replica_groups=mesh['seq'=64,'ch'=8] {'ch'}, use_global_device_ids=true, to_apply=%add.1 | all-reduce | flops 1536 | bytes 12288
  32.0 22.1 %all-gather.5.cloned.1.call-done = bf16[1536,512]{1,0:T(8,128)(2,1)} async-done(((bf16[192,512]{1,0:T(8,128)(2,1)}), bf16[1536,512]{1,0:T(8,128)(2,1)}) %all-gather.5.cloned.1.call-update) | async-done | bytes 1572880 | tf_op jit(solution)/shard_map/all_gather | solution.py:52
  54.1 1.8 convert_reduce_fusion
  56.0 0.5 fusion.2
  56.5 84.5 %all-gather.3.cloned.1.call-done = bf16[1536,384]{1,0:T(8,128)(2,1)} async-done(((bf16[24,384]{1,0:T(8,128)(2,1)}), bf16[1536,384]{1,0:T(8,128)(2,1)}) %all-gather.3.cloned.1.call-update) | async-done | bytes 1179664 | tf_op jit(solution)/shard_map/all_gather | solution.py:60
  141.0 2.1 fusion.29
  143.2 0.1 multiply_convert_fusion.5
  143.3 0.1 fusion.46
  143.4 2.2 collective-permute-start.1
  145.5 3.4 collective-permute-start
  149.0 1.1 collective-permute-done
  150.1 0.8 fusion.33
  151.0 0.4 reshape.57
  151.4 0.4 copy.24
  151.9 2.0 convolution_select_fusion.1
  153.9 1.4 copy.36
  155.3 1.0 reshape.55
  156.3 2.0 multiply_convert_fusion.3
  158.4 6.4 %collective-permute-start.3 = (bf16[192,15]{1,0:T(8,128)(2,1)S(1)}, bf16[192,15]{1,0:T(8,128)(2,1)S(1)}, u32[]{:S(2)}, u32[]{:S(2)}) collective-permute-start(bf16[192,15]{1,0:T(8,128)(2,1)S(1)} %get-tuple-element.18), channel_id=1, source_target_pairs={{8,0},{16,8},{24,16},{32,24},{40,32},{48,40},{56,48},{64,56},{72,6... | collective-permute-start | bytes 17288 | tf_op jit(solution)/shard_map/ppermute | solution.py:17
  164.8 1.9 collective-permute-start.2
  166.8 1.2 collective-permute-done.2
  167.9 0.1 maximum_bitcast_fusion
  168.1 0.4 reshape.58
  168.5 0.4 copy.30
  169.0 2.0 convolution_select_fusion
  171.0 1.4 copy.37
  172.4 1.0 reshape.56
  173.5 1.2 multiply_convert_fusion.2
  174.6 3.4 convolution_convert_fusion
  178.1 0.2 all-reduce.4.cloned.1.call-start
  178.3 2.1 fusion
  180.4 0.9 copy.34
  181.3 0.4 copy.35
  181.7 2.2 fusion.48
  184.0 2.4 fusion.28
  186.4 37.6 %reduce-scatter.2.cloned.1.call-done = bf16[192,512]{1,0:T(8,128)(2,1)} async-done(((bf16[1536,512]{1,0:T(8,128)(2,1)}), bf16[192,512]{1,0:T(8,128)(2,1)}) %reduce-scatter.2.cloned.1.call-update) | async-done | bytes 196624 | tf_op jit(solution)/shard_map/reduce_scatter | solution.py:87
  224.0 1.3 fusion.24
  225.3 3.3 pad_maximum_fusion
  228.6 12.6 %psum.14 = f32[2,512]{1,0:T(2,128)S(1)} all-reduce(f32[2,512]{1,0:T(2,128)S(1)} %pad_maximum_fusion.6), channel_id=1, replica_groups=mesh['seq'=64,'ch'=8] {'ch'}, use_global_device_ids=true, to_apply=%region_5.0 | all-reduce | flops 1024 | bytes 8192 | tf_op jit(solution)/shard_map/psum | solution.py:98
  241.2 1.8 fusion.23
  243.0 190.9 %all-reduce.4.cloned.1.call-done = f32[1568,384]{1,0:T(8,128)} async-done(((f32[1568,384]{1,0:T(8,128)}), f32[1568,384]{1,0:T(8,128)}) %all-reduce.4.cloned.1.call-update) | async-done | bytes 2408464 | tf_op jit(solution)/shard_map/psum | solution.py:106
  433.9 1.4 slice.64
  435.3 1.3 slice.65
  436.5 1.5 fusion.44
  (33 shorter events, 0.5 us)
Async XLA Ops:
  7.2 144.7 %copy-start = (f32[31,192]{1,0:T(8,128)S(1)}, f32[31,192]{1,0:T(8,128)}, u32[]{:S(2)}) copy-start(f32[31,192]{1,0:T(8,128)} %param.10) | copy-start | bytes 71428
  7.2 46.9 %all-gather.5.cloned.1.call-start = ((), (), s32[]{:S(2)}) async-start(), calls=%async_computation.2 | async-start | bytes 1769472 | tf_op jit(solution)/shard_map/all_gather | solution.py:52
  7.9 133.1 %all-gather.3.cloned.1.call-start = ((), (), s32[]{:S(2)}) async-start(), calls=%async_computation.1 | async-start | bytes 1198080 | tf_op jit(solution)/shard_map/all_gather | solution.py:60
  9.4 214.6 %reduce-scatter.2.cloned.1.call-start = ((), (), s32[]{:S(2)}) async-start(), calls=%async_computation.3 | async-start | bytes 1769472 | tf_op jit(solution)/shard_map/reduce_scatter | solution.py:87
  54.1 1.9 copy-start.1
  143.2 8.7 %copy-start.5 = (pred[8,68]{0,1:T(8,128)(4,1)S(1)}, pred[8,68]{0,1:T(8,128)(4,1)}, u32[]{:S(2)}) copy-start(pred[8,68]{0,1:T(8,128)(4,1)} %constant.49) | copy-start | bytes 1636
  143.4 5.6 %collective-permute-start.1 = (bf16[192,15]{1,0:T(8,128)(2,1)S(1)}, bf16[192,15]{1,0:T(8,128)(2,1)S(1)}, u32[]{:S(2)}, u32[]{:S(2)}) collective-permute-start(bf16[192,15]{1,0:T(8,128)(2,1)S(1)} %get-tuple-element.20), channel_id=1, source_target_pairs={{8,0},{16,8},{24,16},{32,24},{40,32},{48,40},{56,48},{64,56},{72,6... | collective-permute-start | bytes 17288 | tf_op jit(solution)/shard_map/ppermute | solution.py:17
  145.5 4.6 %collective-permute-start = (bf16[192,15]{1,0:T(8,128)(2,1)S(1)}, bf16[192,15]{1,0:T(8,128)(2,1)S(1)}, u32[]{:S(2)}, u32[]{:S(2)}) collective-permute-start(bf16[192,15]{1,0:T(8,128)(2,1)S(1)} %get-tuple-element.19), channel_id=1, source_target_pairs={{0,8},{8,16},{16,24},{24,32},{32,40},{40,48},{48,56},{56,64},{64,7... | collective-permute-start | bytes 17288 | tf_op jit(solution)/shard_map/ppermute | solution.py:15
  158.4 8.4 %collective-permute-start.3 = (bf16[192,15]{1,0:T(8,128)(2,1)S(1)}, bf16[192,15]{1,0:T(8,128)(2,1)S(1)}, u32[]{:S(2)}, u32[]{:S(2)}) collective-permute-start(bf16[192,15]{1,0:T(8,128)(2,1)S(1)} %get-tuple-element.18), channel_id=1, source_target_pairs={{8,0},{16,8},{24,16},{32,24},{40,32},{48,40},{56,48},{64,56},{72,6... | collective-permute-start | bytes 17288 | tf_op jit(solution)/shard_map/ppermute | solution.py:17
  164.8 3.1 collective-permute-start.2
  178.0 2.4 copy-start.2
  178.1 255.9 %all-reduce.4.cloned.1.call-start = ((), (), s32[]{:S(2)}) async-start(), calls=%async_computation.4 | async-start | bytes 4816896 | tf_op jit(solution)/shard_map/psum | solution.py:106
  184.0 40.0 %copy-start.4 = (f32[192]{0:T(256)S(1)}, f32[192]{0:T(256)}, u32[]{:S(2)}) copy-start(f32[192]{0:T(256)} %param.7) | copy-start | bytes 2308
  228.6 12.6 %copy-start.3 = (bf16[192,512]{1,0:T(8,128)(2,1)S(1)}, bf16[192,512]{1,0:T(8,128)(2,1)}, u32[]{:S(2)}) copy-start(bf16[192,512]{1,0:T(8,128)(2,1)} %reduce-scatter.2.cloned.1.call-done) | copy-start | bytes 589828
Sparse Core Ops, SparseCore 0:
  10.1 43.9 all-gather.4
  57.9 83.0 all-gather.2
  178.2 45.7 reduce-scatter.1
  228.7 205.1 all-reduce.3
where the time goes:
time: 445 us
  waiting for transfers between devices  338 us (76%)
  blocking collectives  32.2 us (7%)
  other arithmetic  16.4 us (4%)
  between operations  14.7 us (3%)
  local copies, waits for them, and re-layouts  14.5 us (3%)
  starting transfers between devices  14.3 us (3%)
  matrix products  14.2 us (3%)
    psum x1, waiting for transfers between devices, shards(): summed = lax.psum(jnp.concatenate([weight_partial, extra], 0), 'seq')  191 us
    all_gather x1, waiting for transfers between devices, shards(): gathered = lax.all_gather(stacked, 'seq', axis=0, tiled=True)  84.5 us
    reduce_scatter x1, waiting for transfers between devices, shards(): lax.psum_scatter(normed_term.astype(jnp.bfloat16), 'ch', scatter_dimensio...  37.6 us
    all_gather x1, waiting for transfers between devices, shards(): complete_signal = lax.all_gather(signal, 'ch', axis=0, tiled=True)  22.1 us
    unnamed x1, blocking collectives  19.7 us
    psum x1, blocking collectives, shards(): moments = lax.psum(moments, 'ch') * (1.0 / complete_signal.shape[0])  12.6 us
  transfers between devices with their start and end apart: 8, of which 6 were waited for; matrix products, arithmetic and copies ran while one was open for 4% of the time, Pallas kernels for 0%

commit v1 on v0

--- a/solution.py
+++ b/solution.py
@@ -49,7 +49,8 @@
     seq_position = lax.axis_index("seq")
     channel_position = lax.axis_index("ch")
     reach = depth_taps.shape[0] // 2
-    complete_signal = lax.all_gather(signal, "ch", axis=0, tiled=True)
+    sent = jnp.stack([signal] * lax.axis_size("ch"))
+    complete_signal = jnp.concatenate(lax.all_to_all(sent, "ch", 0, 0), axis=0)
     complete_gain = lax.all_gather(input_norm_gain, "ch", axis=0, tiled=True)
     centered_unit, inverse_deviation = standardize_rows(complete_signal)
     normalized_signal = (centered_unit * complete_gain[:, None]).astype(jnp.bfloat16)

time: 445 us -> 410 us (0.921)
  waiting for transfers between devices: 338 us -> 271 us
  blocking collectives: 32.2 us -> 54.6 us
  starting transfers between devices: 14.3 us -> 24.2 us
    all_gather x1, waiting for transfers between devices: 84.5 us -> 38.8 us  [shards(): gathered = lax.all_gather(stacked, 'seq', axis=0, tiled=True)]
    unnamed x1, blocking collectives: 19.7 us -> 42.5 us
    all_gather x1 -> x0, waiting for transfers between devices: 22.1 us -> none  [shards(): complete_signal = lax.all_gather(signal, 'ch', axis=0, tiled=True)]
    all_to_all x0 -> x1, starting transfers between devices: none -> 10 us  [shards(): complete_signal = jnp.concatenate(lax.all_to_all(sent, 'ch', 0, 0), axis=0)]
  transfers between devices with their start and end apart: 8 -> 8, of which waited for: 6 -> 5; matrix products, arithmetic and copies ran while one was open for 4% -> 3% of each run, Pallas kernels for 0% -> 0%
where the time goes in v1:
time: 410 us
  waiting for transfers between devices  271 us (66%)
  blocking collectives  54.6 us (13%)
  starting transfers between devices  24.2 us (6%)
  local copies, waits for them, and re-layouts  16.1 us (4%)
  between operations  14.7 us (4%)
  other arithmetic  14.2 us (3%)
  matrix products  14.2 us (3%)
    psum x1, waiting for transfers between devices, shards(): summed = lax.psum(jnp.concatenate([weight_partial, extra], 0), 'seq')  190 us
    unnamed x1, blocking collectives  42.5 us
    reduce_scatter x1, waiting for transfers between devices, shards(): lax.psum_scatter(normed_term.astype(jnp.bfloat16), 'ch', scatter_dimensio...  39.7 us
    all_gather x1, waiting for transfers between devices, shards(): gathered = lax.all_gather(stacked, 'seq', axis=0, tiled=True)  38.8 us
    psum x1, blocking collectives, shards(): moments = lax.psum(moments, 'ch') * (1.0 / complete_signal.shape[0])  12.1 us
    all_to_all x1, starting transfers between devices, shards(): complete_signal = jnp.concatenate(lax.all_to_all(sent, 'ch', 0, 0), axis=0)  10 us
    ppermute x2, starting transfers between devices, extended(): lax.ppermute(head, axis, [((i + 1) % count, i) for i in range(ends)])  8.58 us
  transfers between devices with their start and end apart: 8, of which 5 were waited for; matrix products, arithmetic and copies ran while one was open for 3% of the time, Pallas kernels for 0%

profile of v1, /device:TPU:25, one launch (start us, length us, event | category | flops | bytes accessed | tf_op | source)
XLA Modules:
  0.0 409.5 jit_solution(5130993227094594396)
XLA Ops:
  7.2 2.2 stack.2
  9.5 10.0 %all-to-all-start = ((bf16[8,192,512]{2,1,0:T(8,128)(2,1)}), bf16[8,192,512]{2,1,0:T(8,128)(2,1)S(1)}, u32[]{:S(2)}, u32[]{:S(2)}) async-start(bf16[8,192,512]{2,1,0:T(8,128)(2,1)} %stack.2), calls=%async_computation | async-start | bytes 3145728 | tf_op jit(solution)/shard_map/all_to_all | solution.py:53
  19.6 0.7 pad_maximum_fusion.5
  20.3 1.3 dynamic-slice
  22.3 0.3 dynamic-update-slice
  22.6 42.5 %all-reduce.1 = f32[1536]{0:T(1024)S(1)} all-reduce(f32[1536]{0:T(1024)S(1)} %dynamic-update-slice), channel_id=1, replica_groups=mesh['seq'=64,'ch'=8] {'ch'}, use_global_device_ids=true, to_apply=%add.1 | all-reduce | flops 1536 | bytes 12288
  65.1 0.3 convert_reduce_fusion
  65.4 0.5 multiply_reduce_fusion
  65.9 2.1 fusion
  68.0 38.8 %all-gather.2.cloned.1.call-done = bf16[1536,384]{1,0:T(8,128)(2,1)} async-done(((bf16[24,384]{1,0:T(8,128)(2,1)}), bf16[1536,384]{1,0:T(8,128)(2,1)}) %all-gather.2.cloned.1.call-update) | async-done | bytes 1179664 | tf_op jit(solution)/shard_map/all_gather | solution.py:61
  106.8 2.1 fusion.46
  108.9 0.1 multiply_convert_fusion.5
  109.0 0.1 fusion.43
  109.1 2.1 collective-permute-start.1
  111.2 3.4 collective-permute-start
  114.7 1.1 collective-permute-done
  115.8 0.9 fusion.30
  116.7 0.4 reshape.68
  117.1 0.4 copy.24
  117.6 2.0 convolution_select_fusion.1
  119.6 1.4 copy.36
  121.0 1.0 reshape.66
  122.1 2.0 multiply_convert_fusion.3
  124.1 6.4 %collective-permute-start.3 = (bf16[192,15]{1,0:T(8,128)(2,1)S(1)}, bf16[192,15]{1,0:T(8,128)(2,1)S(1)}, u32[]{:S(2)}, u32[]{:S(2)}) collective-permute-start(bf16[192,15]{1,0:T(8,128)(2,1)S(1)} %get-tuple-element.20), channel_id=1, source_target_pairs={{8,0},{16,8},{24,16},{32,24},{40,32},{48,40},{56,48},{64,56},{72,6... | collective-permute-start | bytes 17288 | tf_op jit(solution)/shard_map/ppermute | solution.py:17
  130.5 1.9 collective-permute-start.2
  132.5 1.2 collective-permute-done.2
  133.7 0.1 maximum_bitcast_fusion
  133.9 0.4 reshape.69
  134.3 0.4 copy.30
  134.7 2.0 convolution_select_fusion
  136.7 1.4 copy.37
  138.2 1.0 reshape.67
  139.2 1.2 multiply_convert_fusion.2
  140.4 3.4 convolution_convert_fusion
  143.8 0.2 all-reduce.4.cloned.1.call-start
  144.1 0.9 copy.34
  145.0 0.4 copy.35
  145.4 2.2 fusion.45
  147.7 2.4 fusion.26
  150.1 39.7 %reduce-scatter.2.cloned.1.call-done = bf16[192,512]{1,0:T(8,128)(2,1)} async-done(((bf16[1536,512]{1,0:T(8,128)(2,1)}), bf16[192,512]{1,0:T(8,128)(2,1)}) %reduce-scatter.2.cloned.1.call-update) | async-done | bytes 196624 | tf_op jit(solution)/shard_map/reduce_scatter | solution.py:88
  189.8 1.3 fusion.22
  191.1 3.3 pad_maximum_fusion
  194.5 12.1 %psum.14 = f32[2,512]{1,0:T(2,128)S(1)} all-reduce(f32[2,512]{1,0:T(2,128)S(1)} %pad_maximum_fusion.6), channel_id=1, replica_groups=mesh['seq'=64,'ch'=8] {'ch'}, use_global_device_ids=true, to_apply=%region_5.0 | all-reduce | flops 1024 | bytes 8192 | tf_op jit(solution)/shard_map/psum | solution.py:99
  206.6 1.8 fusion.21
  208.4 190.5 %all-reduce.4.cloned.1.call-done = f32[1568,384]{1,0:T(8,128)} async-done(((f32[1568,384]{1,0:T(8,128)}), f32[1568,384]{1,0:T(8,128)}) %all-reduce.4.cloned.1.call-update) | async-done | bytes 2408464 | tf_op jit(solution)/shard_map/psum | solution.py:107
  398.9 1.4 slice.64
  400.2 1.3 slice.65
  401.5 1.5 fusion.41
  (35 shorter events, 0.4 us)
Async XLA Ops:
  7.2 110.4 %copy-start = (f32[31,192]{1,0:T(8,128)S(1)}, f32[31,192]{1,0:T(8,128)}, u32[]{:S(2)}) copy-start(f32[31,192]{1,0:T(8,128)} %param.10) | copy-start | bytes 71428
  7.2 12.4 %copy-start.3 = (bf16[24,192]{1,0:T(8,128)(2,1)S(1)}, bf16[24,192]{1,0:T(8,128)(2,1)}, u32[]{:S(2)}) copy-start(bf16[24,192]{1,0:T(8,128)(2,1)} %param.9) | copy-start | bytes 27652
  7.2 12.4 %copy-start.4 = (bf16[24,192]{1,0:T(8,128)(2,1)S(1)}, bf16[24,192]{1,0:T(8,128)(2,1)}, u32[]{:S(2)}) copy-start(bf16[24,192]{1,0:T(8,128)(2,1)} %param.8) | copy-start | bytes 27652
  7.2 15.1 %copy-start.5 = (f32[192]{0:T(256)S(1)}, f32[192]{0:T(256)}, u32[]{:S(2)}) copy-start(f32[192]{0:T(256)} %param.7) | copy-start | bytes 2308
  9.5 55.6 %all-to-all-start = ((bf16[8,192,512]{2,1,0:T(8,128)(2,1)}), bf16[8,192,512]{2,1,0:T(8,128)(2,1)S(1)}, u32[]{:S(2)}, u32[]{:S(2)}) async-start(bf16[8,192,512]{2,1,0:T(8,128)(2,1)} %stack.2), calls=%async_computation | async-start | bytes 3145728 | tf_op jit(solution)/shard_map/all_to_all | solution.py:53
  19.5 87.3 %all-gather.2.cloned.1.call-start = ((), (), s32[]{:S(2)}) async-start(), calls=%async_computation.2 | async-start | bytes 1198080 | tf_op jit(solution)/shard_map/all_gather | solution.py:61
  20.3 169.6 %reduce-scatter.2.cloned.1.call-start = ((), (), s32[]{:S(2)}) async-start(), calls=%async_computation.3 | async-start | bytes 1769472 | tf_op jit(solution)/shard_map/reduce_scatter | solution.py:88
  108.9 8.7 %copy-start.6 = (pred[8,68]{0,1:T(8,128)(4,1)S(1)}, pred[8,68]{0,1:T(8,128)(4,1)}, u32[]{:S(2)}) copy-start(pred[8,68]{0,1:T(8,128)(4,1)} %constant.49) | copy-start | bytes 1636
  109.1 5.6 %collective-permute-start.1 = (bf16[192,15]{1,0:T(8,128)(2,1)S(1)}, bf16[192,15]{1,0:T(8,128)(2,1)S(1)}, u32[]{:S(2)}, u32[]{:S(2)}) collective-permute-start(bf16[192,15]{1,0:T(8,128)(2,1)S(1)} %get-tuple-element.22), channel_id=1, source_target_pairs={{8,0},{16,8},{24,16},{32,24},{40,32},{48,40},{56,48},{64,56},{72,6... | collective-permute-start | bytes 17288 | tf_op jit(solution)/shard_map/ppermute | solution.py:17
  111.2 4.6 %collective-permute-start = (bf16[192,15]{1,0:T(8,128)(2,1)S(1)}, bf16[192,15]{1,0:T(8,128)(2,1)S(1)}, u32[]{:S(2)}, u32[]{:S(2)}) collective-permute-start(bf16[192,15]{1,0:T(8,128)(2,1)S(1)} %get-tuple-element.21), channel_id=1, source_target_pairs={{0,8},{8,16},{16,24},{24,32},{32,40},{40,48},{48,56},{56,64},{64,7... | collective-permute-start | bytes 17288 | tf_op jit(solution)/shard_map/ppermute | solution.py:15
  124.1 8.4 %collective-permute-start.3 = (bf16[192,15]{1,0:T(8,128)(2,1)S(1)}, bf16[192,15]{1,0:T(8,128)(2,1)S(1)}, u32[]{:S(2)}, u32[]{:S(2)}) collective-permute-start(bf16[192,15]{1,0:T(8,128)(2,1)S(1)} %get-tuple-element.20), channel_id=1, source_target_pairs={{8,0},{16,8},{24,16},{32,24},{40,32},{48,40},{56,48},{64,56},{72,6... | collective-permute-start | bytes 17288 | tf_op jit(solution)/shard_map/ppermute | solution.py:17
  130.5 3.1 collective-permute-start.2
  140.4 3.7 copy-start.1
  143.8 255.0 %all-reduce.4.cloned.1.call-start = ((), (), s32[]{:S(2)}) async-start(), calls=%async_computation.4 | async-start | bytes 4816896 | tf_op jit(solution)/shard_map/psum | solution.py:107
  194.4 12.1 %copy-start.2 = (bf16[192,512]{1,0:T(8,128)(2,1)S(1)}, bf16[192,512]{1,0:T(8,128)(2,1)}, u32[]{:S(2)}) copy-start(bf16[192,512]{1,0:T(8,128)(2,1)} %reduce-scatter.2.cloned.1.call-done) | copy-start | bytes 589828
Sparse Core Ops, SparseCore 0:
  24.2 82.5 all-gather.1
  144.0 45.8 reduce-scatter.1
  194.6 204.2 all-reduce.3
